TPU v7x, 32 devices: a whole 2x2x4 slice. The times are simulated.
32 devices in a mesh: img: 4 (over z), ref: 8 (over y, x, core).
Axes of the slice: x: 2, y: 2, z: 4, core: 2. Of those that a mesh axis runs over, the one named last changes fastest.
Arguments:
- images: bfloat16 [2048, 9216], P(('img', 'ref')), may hold values from -96 to 96
- references: bfloat16 [6912, 9216], P('ref'), may hold values from -0.5 to 0.5
- class_prior: float32 [192], P('ref'), may hold values from 0.2 to 5
Outputs:
- class_sums: float32 [192, 9216], P('ref', 'img')
- class_weights: float32 [192], P('ref')
All inputs are finite; a program needn't handle non-finite values.
Results may differ from a plain program's by a relative error of at most 0.0021.
Values may be sent and summed in bfloat16 or wider, within the bound.
No kernel may reach another device: no remote copies, remote signals or barrier semaphores. Data moves between devices by JAX's collectives and lax.ppermute only.
A program may use at most 128 MiB of HBM per device.

v0:
```python
import jax
import jax.numpy as jnp
from jax import lax
from jax.sharding import PartitionSpec as P

ANG = 144


def unturn(stacked, shift_size):
    classes_here, rotations, columns = stacked.shape
    cycles = stacked.reshape(classes_here, rotations, columns // ANG, ANG)
    doubled = jnp.concatenate([cycles, cycles], axis=3)
    result = doubled[:, 0, :, 0:ANG]
    for turn_index in range(1, rotations):
        start_col = turn_index * shift_size
        result = result + doubled[:, turn_index, :, start_col : start_col + ANG]
    return result.reshape(classes_here, columns)


def per_device(images, references, class_prior):
    local_refs, pixels = references.shape
    classes_here = class_prior.shape[0]
    rotations = local_refs // classes_here
    shift_size = ANG // rotations
    half_norm = 0.5 * jnp.einsum(
        "jp,jp->j", references, references, preferred_element_type=jnp.float32
    )
    offsets = (jnp.log(class_prior)[:, None] - half_norm.reshape(classes_here, rotations)).reshape(
        local_refs
    )
    gathered = lax.all_gather(images, "ref", axis=0, tiled=True)
    products = lax.dot_general(
        gathered, references, (((1,), (1,)), ((), ())), preferred_element_type=jnp.float32
    )
    scores = products + offsets
    local_max = jnp.max(scores, axis=1)
    top_score = lax.pmax(local_max, "ref")
    denominator = lax.psum(jnp.sum(jnp.exp(scores - top_score[:, None]), axis=1), "ref")
    weights = (jnp.exp(scores - top_score[:, None]) / denominator[:, None]).astype(jnp.bfloat16)
    local_mass = (
        jnp.sum(weights.astype(jnp.float32), axis=0).reshape(classes_here, rotations).sum(axis=1)
    )
    class_weights = lax.psum(local_mass, "img")
    sums = lax.dot_general(
        weights, gathered, (((0,), (0,)), ((), ())), preferred_element_type=jnp.float32
    )
    reduced = lax.psum_scatter(sums, "img", scatter_dimension=1, tiled=True)
    class_sums = unturn(reduced.reshape(classes_here, rotations, -1), shift_size)
    return (class_sums, class_weights)


def solution(mesh):
    placed = (P(("img", "ref"), None), P("ref", None), P("ref"))
    return jax.shard_map(
        per_device,
        mesh=mesh,
        in_specs=placed,
        out_specs=(P("ref", "img"), P("ref")),
        check_vma=False,
    )
```

profile of v0, /device:TPU:0, one launch (start us, length us, event | category | flops | bytes accessed | tf_op | source)
XLA Modules:
  0.0 719.0 jit_solution(10911316544609606139)
XLA Ops:
  8.8 7.0 fusion
  15.8 55.7 %all-gather.2.cloned.1.call-done = bf16[512,9216]{1,0:T(8,128)(2,1)} async-done(((bf16[64,9216]{1,0:T(8,128)(2,1)}), bf16[512,9216]{1,0:T(8,128)(2,1)}) %all-gather.2.cloned.1.call-update) | async-done | bytes 9437200 | tf_op jit(solution)/shard_map/all_gather | solution.py:31
  71.4 14.2 %add_reduce_fusion = (f32[512]{0:T(512)S(1)}, f32[512,864]{0,1:T(8,128)S(1)}) fusion(f32[864]{0:T(1024)S(1)} %multiply_subtract_fusion, bf16[512,9216]{1,0:T(8,128)(2,1)} %all-gather.2.cloned.1.call-done, bf16[864,9216]{1,0:T(8,128)(2,1)} %param.4), kind=kOutput, calls=%fused_computation.5 | convolution fusion | flops 8154611200 | bytes 27137408 | tf_op jit(solution)/shard_map/dot_general | solution.py:32
  85.6 13.1 %pmax.7 = f32[512]{0:T(512)S(1)} all-reduce(f32[512]{0:T(512)S(1)} %get-tuple-element.22), channel_id=1, replica_groups=mesh['img'=4,'ref'=8] {'ref'}, use_global_device_ids=true, to_apply=%region_1.0 | all-reduce | flops 512 | bytes 4096 | tf_op jit(solution)/shard_map/pmax | solution.py:37
  99.1 11.8 %psum.14 = f32[512]{0:T(512)S(1)} all-reduce(f32[512]{0:T(512)S(1)} %fusion.1), channel_id=1, replica_groups=mesh['img'=4,'ref'=8] {'ref'}, use_global_device_ids=true, to_apply=%region_3.0 | all-reduce | flops 512 | bytes 4096 | tf_op jit(solution)/shard_map/psum | solution.py:38
  111.4 17.6 %fusion.2 = f32[864,9216]{1,0:T(8,128)} fusion(bf16[512,864]{0,1:T(8,128)(2,1)S(1)} %get-tuple-element.3, bf16[512,9216]{1,0:T(8,128)(2,1)} %all-gather.2.cloned.1.call-done), kind=kOutput, calls=%fused_computation.44 | convolution fusion | flops 8153726976 | bytes 42172416 | tf_op jit(solution)/shard_map/dot_general | solution.py:44
  129.2 12.4 %psum.15 = f32[24]{0:T(128)} all-reduce(f32[24]{0:T(128)S(1)} %reduce_sum.29), channel_id=1, replica_groups=mesh['img'=4,'ref'=8] {'img'}, use_global_device_ids=true, to_apply=%region_7.0 | all-reduce | flops 24 | bytes 192 | tf_op jit(solution)/shard_map/psum | solution.py:43
  141.6 513.8 %reduce-scatter.2.cloned.1.call-done = f32[864,2304]{1,0:T(8,128)} async-done(((f32[864,9216]{1,0:T(8,128)}), f32[864,2304]{1,0:T(8,128)}) %reduce-scatter.2.cloned.1.call-update) | async-done | bytes 7962640 | tf_op jit(solution)/shard_map/reduce_scatter | solution.py:47
  655.4 15.2 %reshape_reshape.3 = f32[24,36,16,144]{3,2,1,0:T(8,128)} reshape(f32[864,2304]{1,0:T(8,128)} %reduce-scatter.2.cloned.1.call-done) | data formatting | bytes 15925248 | tf_op jit(solution)/shard_map/reshape;reshape | solution.py:11
  670.6 8.5 %maximum_add_fusion = f32[24,1,16,144]{3,2,1,0:T(8,128)} fusion(f32[24,36,16,144]{3,2,1,0:T(8,128)} %reshape_reshape.3), kind=kLoop, calls=%fused_computation.26 | loop fusion | flops 1769472 | bytes 14770176 | tf_op jit(solution)/shard_map/add | solution.py:16
  680.2 3.5 pad_maximum_fusion.18
  683.7 2.5 pad_maximum_fusion.17
  686.2 1.9 reshape.71
  688.1 1.9 squeeze.128
  690.0 1.9 squeeze.111
  691.9 1.9 squeeze.110
  693.8 1.9 squeeze.126
  695.6 1.9 squeeze.118
  697.5 1.9 squeeze.122
  699.4 1.9 squeeze.117
  701.3 1.9 squeeze.124
  703.2 1.9 squeeze.116
  705.1 1.9 squeeze.121
  709.5 2.7 add_add_fusion
  (24 shorter events, 6.4 us)
Async XLA Ops:
  7.2 64.3 %all-gather.2.cloned.1.call-start = ((), (), s32[]{:S(2)}) async-start(), calls=%async_computation.1 | async-start | bytes 10616832 | tf_op jit(solution)/shard_map/all_gather | solution.py:31
  7.9 647.5 %reduce-scatter.2.cloned.1.call-start = ((), (), s32[]{:S(2)}) async-start(), calls=%async_computation.2 | async-start | bytes 39813120 | tf_op jit(solution)/shard_map/reduce_scatter | solution.py:47
  670.6 8.6 %copy-start = (f32[24,36,16,144]{3,2,1,0:T(8,128)S(1)}, f32[24,36,16,144]{3,2,1,0:T(8,128)}, u32[]{:S(2)}) copy-start(f32[24,36,16,144]{3,2,1,0:T(8,128)} %reshape_reshape.3) | copy-start | bytes 23887876
Sparse Core Ops, SparseCore 0:
  9.9 61.5 all-gather.1
  129.1 526.1 reduce-scatter.1
where the time goes:
time: 720 us; the launch traced here: 719 us
  waiting for transfers between devices  570 us (79%)
  local copies, waits for them, and re-layouts  39.7 us (6%)
  blocking collectives  37.3 us (5%)
  matrix products  31.7 us (4%)
  other arithmetic  26.1 us (4%)
  between operations  14.1 us (2%)
    reduce_scatter x1, waiting for transfers between devices, per_device(): reduced = lax.psum_scatter(sums, 'img', scatter_dimension=1, tiled=True)  514 us
    all_gather x1, waiting for transfers between devices, per_device(): gathered = lax.all_gather(images, 'ref', axis=0, tiled=True)  55.7 us
    squeeze x19, local copies, waits for them, and re-layouts, unturn(): result = result + doubled[:, turn_index, :, start_col:start_col + ANG]  21.4 us
    dot_general x1, matrix products, per_device(): lax.dot_general(weights, gathered, (((0,), (0,)), ((), ())), preferred_el...  17.6 us
    another operation x1, local copies, waits for them, and re-layouts, unturn(): cycles = stacked.reshape(classes_here, rotations, columns // ANG, ANG)  15.2 us
  transfers between devices with their start and end apart: 2, of which 2 were waited for; matrix products, arithmetic and copies ran while one was open for 1% of the time, Pallas kernels for 0%

commit v1 on v0

--- a/solution.py
+++ b/solution.py
@@ -4,6 +4,12 @@
 from jax.sharding import PartitionSpec as P
 
 ANG = 144
+
+
+def laid_out(blocks, dim):
+    blocks = jnp.moveaxis(blocks, 0, dim)
+    shape = blocks.shape
+    return blocks.reshape(*shape[:dim], shape[dim] * shape[dim + 1], *shape[dim + 2 :])
 
 
 def unturn(stacked, shift_size):
@@ -28,7 +34,19 @@
     offsets = (jnp.log(class_prior)[:, None] - half_norm.reshape(classes_here, rotations)).reshape(
         local_refs
     )
-    gathered = lax.all_gather(images, "ref", axis=0, tiled=True)
+    length = lax.axis_size("ref")
+    pairs = [(i, (i + 1) % length) for i in range(length)]
+    back = [(b, a) for a, b in pairs]
+    lower, upper = ([], [])
+    for turn in range(length - 1):
+        if turn % 2 == 0:
+            lower.append(lax.ppermute(lower[-1] if lower else images, "ref", pairs))
+        else:
+            upper.append(lax.ppermute(upper[-1] if upper else images, "ref", back))
+    blocks = jnp.stack([*lower[::-1], images, *upper])
+    shift = lax.axis_index("ref") - len(lower)
+    blocks = blocks[(jnp.arange(length) - shift) % length]
+    gathered = laid_out(blocks, 0)
     products = lax.dot_general(
         gathered, references, (((1,), (1,)), ((), ())), preferred_element_type=jnp.float32
     )

time: 720 us -> 775 us (1.076)
  waiting for transfers between devices: 570 us -> 596 us
  local copies, waits for them, and re-layouts: 39.7 us -> 58.6 us
  starting transfers between devices: 0.08 us -> 8.58 us
    ppermute x0 -> x7, waiting for transfers between devices: none -> 81.3 us  [the longest x4 81.3 us: per_device(): lower.append(lax.ppermute(lower[-1] if lower else images, 'ref', pairs))]
    all_gather x1 -> x0, waiting for transfers between devices: 55.7 us -> none  [per_device(): gathered = lax.all_gather(images, 'ref', axis=0, tiled=True)]
    unnamed x2 -> x11, local copies, waits for them, and re-layouts: 0.17 us -> 9.14 us
    gather x0 -> x1, local copies, waits for them, and re-layouts: none -> 8.78 us  [per_device(): blocks = blocks[(jnp.arange(length) - shift) % length]]
    ppermute x0 -> x7, starting transfers between devices: none -> 8.54 us  [the longest x3 8.03 us: per_device(): upper.append(lax.ppermute(upper[-1] if upper else images, 'ref', back))]
  transfers between devices with their start and end apart: 2 -> 8, of which waited for: 2 -> 5; matrix products, arithmetic and copies ran while one was open for 1% -> 2% of each run, Pallas kernels for 0% -> 0%
where the time goes in v1:
time: 775 us; the launch traced here: 774 us
  waiting for transfers between devices  596 us (77%)
  local copies, waits for them, and re-layouts  58.6 us (8%)
  blocking collectives  38.7 us (5%)
  matrix products  31.7 us (4%)
  other arithmetic  26.1 us (3%)
  between operations  14.1 us (2%)
  starting transfers between devices  8.58 us (1%)
    reduce_scatter x1, waiting for transfers between devices, per_device(): reduced = lax.psum_scatter(sums, 'img', scatter_dimension=1, tiled=True)  515 us
    ppermute x4, waiting for transfers between devices, per_device(): lower.append(lax.ppermute(lower[-1] if lower else images, 'ref', pairs))  81.3 us
    squeeze x19, local copies, waits for them, and re-layouts, unturn(): result = result + doubled[:, turn_index, :, start_col:start_col + ANG]  21.4 us
    dot_general x1, matrix products, per_device(): lax.dot_general(weights, gathered, (((0,), (0,)), ((), ())), preferred_el...  17.6 us
  transfers between devices with their start and end apart: 8, of which 5 were waited for; matrix products, arithmetic and copies ran while one was open for 2% of the time, Pallas kernels for 0%

profile of v1, /device:TPU:0, one launch (start us, length us, event | category | flops | bytes accessed | tf_op | source)
XLA Modules:
  0.0 773.9 jit_solution(7398608951243656478)
XLA Ops:
  7.7 17.0 %collective-permute-done = bf16[64,9216]{1,0:T(8,128)(2,1)S(1)} collective-permute-done((bf16[64,9216]{1,0:T(8,128)(2,1)}, bf16[64,9216]{1,0:T(8,128)(2,1)S(1)}, u32[]{:S(2)}, u32[]{:S(2)}) %collective-permute-start) | collective-permute-done | bytes 1179680 | tf_op jit(solution)/shard_map/ppermute | solution.py:43
  24.7 2.6 collective-permute-start.4
  27.3 24.5 %collective-permute-done.1 = bf16[64,9216]{1,0:T(8,128)(2,1)S(1)} collective-permute-done((bf16[64,9216]{1,0:T(8,128)(2,1)S(1)}, bf16[64,9216]{1,0:T(8,128)(2,1)S(1)}, u32[]{:S(2)}, u32[]{:S(2)}) %collective-permute-start.1) | collective-permute-done | bytes 1179680 | tf_op jit(solution)/shard_map/ppermute | solution.py:43
  52.8 2.7 collective-permute-start.5
  55.5 24.3 %collective-permute-done.2 = bf16[64,9216]{1,0:T(8,128)(2,1)} collective-permute-done((bf16[64,9216]{1,0:T(8,128)(2,1)S(1)}, bf16[64,9216]{1,0:T(8,128)(2,1)}, u32[]{:S(2)}, u32[]{:S(2)}) %collective-permute-start.2) | collective-permute-done | bytes 1179680 | tf_op jit(solution)/shard_map/ppermute | solution.py:43
  79.7 7.0 fusion
  86.8 2.7 collective-permute-start.6
  89.4 15.5 %collective-permute-done.3 = bf16[64,9216]{1,0:T(8,128)(2,1)S(1)} collective-permute-done((bf16[64,9216]{1,0:T(8,128)(2,1)}, bf16[64,9216]{1,0:T(8,128)(2,1)S(1)}, u32[]{:S(2)}, u32[]{:S(2)}) %collective-permute-start.3) | collective-permute-done | bytes 1179680 | tf_op jit(solution)/shard_map/ppermute | solution.py:43
  106.1 2.4 bitcast_dynamic-update-slice_fusion.6
  115.2 8.8 %gather_fusion = bf16[8,64,9216]{2,1,0:T(8,128)(2,1)} fusion(bf16[8,64,9216]{2,1,0:T(8,128)(2,1)} %bitcast_dynamic-update-slice_fusion, s32[1024]{0:T(1024)S(1)} %pad_clamp_fusion), kind=kCustom, calls=%fused_computation | custom fusion | bytes 18874400 | tf_op jit(solution)/shard_map/gather | solution.py:48
  123.9 14.2 %add_reduce_fusion = (f32[512]{0:T(512)S(1)}, f32[512,864]{0,1:T(8,128)S(1)}) fusion(f32[864]{0:T(1024)S(1)} %multiply_subtract_fusion, bf16[512,9216]{1,0:T(8,128)(2,1)} %bitcast.63, bf16[864,9216]{1,0:T(8,128)(2,1)} %param.4), kind=kOutput, calls=%fused_computation.6 | convolution fusion | flops 8154611200 | bytes 27137408 | tf_op jit(solution)/shard_map/dot_general | solution.py:50
  138.1 11.9 %pmax.7 = f32[512]{0:T(512)S(1)} all-reduce(f32[512]{0:T(512)S(1)} %get-tuple-element.22), channel_id=1, replica_groups=mesh['img'=4,'ref'=8] {'ref'}, use_global_device_ids=true, to_apply=%region_1.2 | all-reduce | flops 512 | bytes 4096 | tf_op jit(solution)/shard_map/pmax | solution.py:55
  150.3 14.3 %psum.14 = f32[512]{0:T(512)S(1)} all-reduce(f32[512]{0:T(512)S(1)} %fusion.1), channel_id=1, replica_groups=mesh['img'=4,'ref'=8] {'ref'}, use_global_device_ids=true, to_apply=%region_3.4 | all-reduce | flops 512 | bytes 4096 | tf_op jit(solution)/shard_map/psum | solution.py:56
  165.2 17.6 %fusion.4 = f32[864,9216]{1,0:T(8,128)} fusion(bf16[512,864]{0,1:T(8,128)(2,1)S(1)} %get-tuple-element.3, bf16[512,9216]{1,0:T(8,128)(2,1)} %bitcast.64), kind=kOutput, calls=%fused_computation.60 | convolution fusion | flops 8153726976 | bytes 42172416 | tf_op jit(solution)/shard_map/dot_general | solution.py:62
  183.0 12.6 %psum.15 = f32[24]{0:T(128)} all-reduce(f32[24]{0:T(128)S(1)} %reduce_sum.29), channel_id=1, replica_groups=mesh['img'=4,'ref'=8] {'img'}, use_global_device_ids=true, to_apply=%region_7.8 | all-reduce | flops 24 | bytes 192 | tf_op jit(solution)/shard_map/psum | solution.py:61
  195.6 514.6 %reduce-scatter.2.cloned.1.call-done = f32[864,2304]{1,0:T(8,128)} async-done(((f32[864,9216]{1,0:T(8,128)}), f32[864,2304]{1,0:T(8,128)}) %reduce-scatter.2.cloned.1.call-update) | async-done | bytes 7962640 | tf_op jit(solution)/shard_map/reduce_scatter | solution.py:65
  710.2 15.2 %reshape_reshape.3 = f32[24,36,16,144]{3,2,1,0:T(8,128)} reshape(f32[864,2304]{1,0:T(8,128)} %reduce-scatter.2.cloned.1.call-done) | data formatting | bytes 15925248 | tf_op jit(solution)/shard_map/reshape;reshape | solution.py:17
  725.4 8.5 %maximum_add_fusion = f32[24,1,16,144]{3,2,1,0:T(8,128)} fusion(f32[24,36,16,144]{3,2,1,0:T(8,128)} %reshape_reshape.3), kind=kLoop, calls=%fused_computation.35 | loop fusion | flops 1769472 | bytes 14770176 | tf_op jit(solution)/shard_map/add | solution.py:22
  735.0 3.5 pad_maximum_fusion.18
  738.5 2.5 pad_maximum_fusion.17
  741.0 1.9 reshape.132
  744.8 1.9 squeeze.111
  754.2 1.9 squeeze.117
  764.3 2.7 add_add_fusion
  (48 shorter events, 29.1 us)
Async XLA Ops:
  7.2 703.0 %reduce-scatter.2.cloned.1.call-start = ((), (), s32[]{:S(2)}) async-start(), calls=%async_computation.1 | async-start | bytes 39813120 | tf_op jit(solution)/shard_map/reduce_scatter | solution.py:65
  7.2 17.5 %collective-permute-start = (bf16[64,9216]{1,0:T(8,128)(2,1)}, bf16[64,9216]{1,0:T(8,128)(2,1)S(1)}, u32[]{:S(2)}, u32[]{:S(2)}) collective-permute-start(bf16[64,9216]{1,0:T(8,128)(2,1)} %param.3), channel_id=1, source_target_pairs={{0,1},{1,2},{2,3},{3,4},{4,5},{5,6},{6,7},{7,0},{8,9},{9,10},{10,1... | collective-permute-start | bytes 3538952 | tf_op jit(solution)/shard_map/ppermute | solution.py:43
  24.7 27.2 %collective-permute-start.1 = (bf16[64,9216]{1,0:T(8,128)(2,1)S(1)}, bf16[64,9216]{1,0:T(8,128)(2,1)S(1)}, u32[]{:S(2)}, u32[]{:S(2)}) collective-permute-start(bf16[64,9216]{1,0:T(8,128)(2,1)S(1)} %collective-permute-done), channel_id=1, source_target_pairs={{0,1},{1,2},{2,3},{3,4},{4,5},{5,6},{6,7},{7,0},{8,9},{9,10},{10,1... | collective-permute-start | bytes 3538952 | tf_op jit(solution)/shard_map/ppermute | solution.py:43
  24.7 28.1 %collective-permute-start.4 = (bf16[64,9216]{1,0:T(8,128)(2,1)}, bf16[64,9216]{1,0:T(8,128)(2,1)S(1)}, u32[]{:S(2)}, u32[]{:S(2)}) collective-permute-start(bf16[64,9216]{1,0:T(8,128)(2,1)} %param.3), channel_id=1, source_target_pairs={{1,0},{2,1},{3,2},{4,3},{5,4},{6,5},{7,6},{0,7},{9,8},{10,9},{11,1... | collective-permute-start | bytes 3538952 | tf_op jit(solution)/shard_map/ppermute | solution.py:45
  51.9 27.9 %collective-permute-start.2 = (bf16[64,9216]{1,0:T(8,128)(2,1)S(1)}, bf16[64,9216]{1,0:T(8,128)(2,1)}, u32[]{:S(2)}, u32[]{:S(2)}) collective-permute-start(bf16[64,9216]{1,0:T(8,128)(2,1)S(1)} %collective-permute-done.1), channel_id=1, source_target_pairs={{0,1},{1,2},{2,3},{3,4},{4,5},{5,6},{6,7},{7,0},{8,9},{9,10},{10,1... | collective-permute-start | bytes 3538952 | tf_op jit(solution)/shard_map/ppermute | solution.py:43
  52.8 57.9 %copy-start.1 = (bf16[64,9216]{1,0:T(8,128)(2,1)S(1)}, bf16[64,9216]{1,0:T(8,128)(2,1)}, u32[]{:S(2)}) copy-start(bf16[64,9216]{1,0:T(8,128)(2,1)} %param.3) | copy-start | bytes 3538948
  52.8 34.0 %collective-permute-start.5 = (bf16[64,9216]{1,0:T(8,128)(2,1)S(1)}, bf16[64,9216]{1,0:T(8,128)(2,1)S(1)}, u32[]{:S(2)}, u32[]{:S(2)}) collective-permute-start(bf16[64,9216]{1,0:T(8,128)(2,1)S(1)} %collective-permute-done.4), channel_id=1, source_target_pairs={{1,0},{2,1},{3,2},{4,3},{5,4},{6,5},{7,6},{0,7},{9,8},{10,9},{11,1... | collective-permute-start | bytes 3538952 | tf_op jit(solution)/shard_map/ppermute | solution.py:45
  79.7 25.2 %collective-permute-start.3 = (bf16[64,9216]{1,0:T(8,128)(2,1)}, bf16[64,9216]{1,0:T(8,128)(2,1)S(1)}, u32[]{:S(2)}, u32[]{:S(2)}) collective-permute-start(bf16[64,9216]{1,0:T(8,128)(2,1)} %collective-permute-done.2), channel_id=1, source_target_pairs={{0,1},{1,2},{2,3},{3,4},{4,5},{5,6},{6,7},{7,0},{8,9},{9,10},{10,1... | collective-permute-start | bytes 3538952 | tf_op jit(solution)/shard_map/ppermute | solution.py:43
  86.8 27.2 %collective-permute-start.6 = (bf16[64,9216]{1,0:T(8,128)(2,1)S(1)}, bf16[64,9216]{1,0:T(8,128)(2,1)S(1)}, u32[]{:S(2)}, u32[]{:S(2)}) collective-permute-start(bf16[64,9216]{1,0:T(8,128)(2,1)S(1)} %collective-permute-done.5), channel_id=1, source_target_pairs={{1,0},{2,1},{3,2},{4,3},{5,4},{6,5},{7,6},{0,7},{9,8},{10,9},{11,1... | collective-permute-start | bytes 3538952 | tf_op jit(solution)/shard_map/ppermute | solution.py:45
  725.4 8.6 %copy-start = (f32[24,36,16,144]{3,2,1,0:T(8,128)S(1)}, f32[24,36,16,144]{3,2,1,0:T(8,128)}, u32[]{:S(2)}) copy-start(f32[24,36,16,144]{3,2,1,0:T(8,128)} %reshape_reshape.3) | copy-start | bytes 23887876
Sparse Core Ops, SparseCore 0:
  182.9 527.2 reduce-scatter.1
